TPU v7x, 256 devices: a whole 4x4x8 slice. The times are simulated.
256 devices in a mesh: section: 4 (over y), expert: 64 (over x, z, core).
Axes of the slice: x: 4, y: 4, z: 8, core: 2. Of those that a mesh axis runs over, the one named last changes fastest.
Arguments:
- tokens: bfloat16 [1024, 4096], P('expert', 'section'), may hold values from -6 to 6
- cotangent: bfloat16 [1024, 4096], P('expert', 'section'), may hold values from -6 to 6
- routes: int32 [1024, 2], P('expert'), may hold values from 0 to 7, all different within a row; in each aligned block of 16 rows (0 to 15, 16 to 31, ...) at most 6 rows name the same one
- w_router: bfloat16 [4096, 8], P('section'), may hold values from -0.09375 to 0.09375
- w_gate: bfloat16 [64, 4096, 1024], P('expert', None, 'section'), may hold values from -0.09375 to 0.09375
- w_up: bfloat16 [64, 4096, 1024], P('expert', None, 'section'), may hold values from -0.09375 to 0.09375
- w_down: bfloat16 [64, 1024, 4096], P('expert', 'section'), may hold values from -0.0625 to 0.0625
Outputs:
- mixed: bfloat16 [1024, 4096], P('expert', 'section')
- grad_tokens: bfloat16 [1024, 4096], P('expert', 'section')
- grad_router: float32 [4096, 8], P('section')
- grad_gate: bfloat16 [64, 4096, 1024], P('expert', None, 'section')
- grad_up: bfloat16 [64, 4096, 1024], P('expert', None, 'section')
- grad_down: bfloat16 [64, 1024, 4096], P('expert', 'section')
Inputs may be any that keep to these rules, and one draw needn't show every extreme that they name: `routes`: each token names two different experts. Within each aligned block of 16 tokens no expert is named by more than 6 tokens, and in every draw some block has an expert named by exactly 6 tokens.
All inputs are finite; a program needn't handle non-finite values.
Results may differ from a plain program's by a relative error of at most 0.023.
Values may be sent and summed in bfloat16 or wider, within the bound.
No kernel may reach another device: no remote copies, remote signals or barrier semaphores. Data moves between devices by JAX's collectives and lax.ppermute only.
A program may use at most 128 MiB of HBM per device.

v0:
```python
import jax
import jax.numpy as jnp
import numpy as np
from jax import lax
from jax.sharding import Mesh
from jax.sharding import PartitionSpec as P

CAP = 6
LANES = 128
EXPERT_AXES = ("ex", "ez", "ec")


def expert_size():
    size = 1
    for name in EXPERT_AXES:
        size = size * lax.axis_size(name)
    return size


def per_device(tokens, cotangent, routes, w_router, w_gate, w_up, w_down):
    highest = lax.Precision.HIGHEST
    experts = w_router.shape[1]
    groups = expert_size() // experts
    capacity = CAP
    tok_count, width = tokens.shape
    n_section = lax.axis_size("section")
    slot_total = experts * capacity
    partial_logits = jnp.dot(tokens, w_router, preferred_element_type=jnp.float32)
    logits = lax.psum(partial_logits, "section")
    route_hot = routes[:, :, None] == jnp.arange(experts, dtype=jnp.int32)[None, None, :]
    zero_f = jnp.zeros((), jnp.float32)
    chosen = jnp.sum(jnp.where(route_hot, logits[:, None, :], zero_f), axis=2)
    gate_first = 1.0 / (1.0 + jnp.exp(chosen[:, 1] - chosen[:, 0]))
    gate_second = 1.0 / (1.0 + jnp.exp(chosen[:, 0] - chosen[:, 1]))
    counts_flat = route_hot.astype(jnp.int32).reshape(2 * tok_count, experts)
    earlier = jnp.cumsum(counts_flat, axis=0) - counts_flat
    position = jnp.sum(earlier * counts_flat, axis=1).reshape(tok_count, 2)
    slot_row = routes * capacity + position
    slot_ids = jnp.arange(slot_total, dtype=jnp.int32)[None, :]
    pick_first = slot_row[:, 0:1] == slot_ids
    pick_second = slot_row[:, 1:2] == slot_ids
    pick_both = (pick_first | pick_second).astype(jnp.bfloat16)
    x_source = jnp.einsum(
        "ts,td->sd", pick_both, tokens, preferred_element_type=jnp.float32
    ).astype(jnp.bfloat16)
    cot_float = cotangent.astype(jnp.float32)
    scaled_first = (gate_first[:, None] * cot_float).astype(jnp.bfloat16)
    scaled_second = (gate_second[:, None] * cot_float).astype(jnp.bfloat16)
    dy_source = jnp.einsum(
        "ts,td->sd",
        pick_first.astype(jnp.bfloat16),
        scaled_first,
        preferred_element_type=jnp.float32,
    )
    dy_source = dy_source + jnp.einsum(
        "ts,td->sd",
        pick_second.astype(jnp.bfloat16),
        scaled_second,
        preferred_element_type=jnp.float32,
    )
    dy_source = dy_source.astype(jnp.bfloat16)
    both_source = jnp.stack(
        [x_source.reshape(experts, capacity * width), dy_source.reshape(experts, capacity * width)],
        axis=1,
    )
    block_rows = 2 * capacity * width // LANES
    sent = jnp.broadcast_to(
        both_source.reshape(experts, 1, block_rows, LANES), (experts, groups, block_rows, LANES)
    ).reshape(experts * groups, block_rows, LANES)
    received = lax.all_to_all(sent, EXPERT_AXES, 0, 0, tiled=True)
    row_total = received.shape[0] * capacity
    received = received.reshape(-1, 2, capacity, width).transpose(1, 0, 2, 3)
    received = received.reshape(2, row_total, width)
    gathered = lax.all_gather(received, "section", axis=2, tiled=True)
    x_rows = gathered[0]
    dy_rows = gathered[1]
    gate_local = w_gate[0]
    up_local = w_up[0]
    down_local = w_down[0]
    pre_gate = jnp.dot(x_rows, gate_local, preferred_element_type=jnp.float32)
    pre_up = jnp.dot(x_rows, up_local, preferred_element_type=jnp.float32)
    sigmoid_gate = jax.nn.sigmoid(pre_gate)
    activated = pre_gate * sigmoid_gate
    hidden = (activated * pre_up).astype(jnp.bfloat16)
    d_hidden = jnp.einsum("pd,fd->pf", dy_rows, down_local, preferred_element_type=jnp.float32)
    grad_down = jnp.einsum("pf,pd->fd", hidden, dy_rows, preferred_element_type=jnp.float32).astype(
        jnp.bfloat16
    )
    d_pre_gate = (
        d_hidden * pre_up * sigmoid_gate * (1.0 + pre_gate * (1.0 - sigmoid_gate))
    ).astype(jnp.bfloat16)
    d_pre_up = (d_hidden * activated).astype(jnp.bfloat16)
    grad_gate = jnp.einsum(
        "pd,pf->df", x_rows, d_pre_gate, preferred_element_type=jnp.float32
    ).astype(jnp.bfloat16)
    grad_up = jnp.einsum("pd,pf->df", x_rows, d_pre_up, preferred_element_type=jnp.float32).astype(
        jnp.bfloat16
    )
    hid = gate_local.shape[1]
    down_blocks = down_local.reshape(hid, n_section, width)
    gate_blocks = gate_local.reshape(n_section, width, hid)
    up_blocks = up_local.reshape(n_section, width, hid)
    out_piece = jnp.einsum("pf,fsd->spd", hidden, down_blocks, preferred_element_type=jnp.float32)
    dx_piece = jnp.einsum(
        "pf,sdf->spd", d_pre_gate, gate_blocks, preferred_element_type=jnp.float32
    )
    dx_piece = dx_piece + jnp.einsum(
        "pf,sdf->spd", d_pre_up, up_blocks, preferred_element_type=jnp.float32
    )
    pieces = jnp.stack([out_piece, dx_piece], axis=1).astype(jnp.bfloat16)
    pieces = pieces.reshape(n_section * 2 * pieces.shape[2], width)
    reduced = lax.psum_scatter(pieces, "section", scatter_dimension=0, tiled=True)
    n_dev = row_total // capacity
    back = reduced.reshape(2, n_dev, capacity, width).transpose(1, 0, 2, 3)
    back = back.reshape(n_dev, block_rows, LANES)
    returned = lax.all_to_all(back, EXPERT_AXES, 0, 0, tiled=True)
    returned = returned.reshape(experts, groups, 2, capacity, width).astype(jnp.float32)
    folded = jnp.sum(returned, axis=1)
    slot_out = folded[:, 0].reshape(slot_total, width)
    slot_dx = folded[:, 1].reshape(slot_total, width)
    first_float = pick_first.astype(jnp.float32)
    second_float = pick_second.astype(jnp.float32)
    out_first = jnp.dot(first_float, slot_out, precision=highest)
    out_second = jnp.dot(second_float, slot_out, precision=highest)
    mixed = (gate_first[:, None] * out_first + gate_second[:, None] * out_second).astype(
        jnp.bfloat16
    )
    local_inner = jnp.stack(
        [jnp.sum(cot_float * out_first, axis=1), jnp.sum(cot_float * out_second, axis=1)], axis=1
    )
    gate_inner = lax.psum(local_inner, "section")
    d_first = gate_first * gate_second * (gate_inner[:, 0] - gate_inner[:, 1])
    d_logits = jnp.where(route_hot[:, 0, :], d_first[:, None], zero_f) - jnp.where(
        route_hot[:, 1, :], d_first[:, None], zero_f
    )
    dx_expert = jnp.dot(first_float, slot_dx, precision=highest)
    dx_expert = dx_expert + jnp.dot(second_float, slot_dx, precision=highest)
    router_float = w_router.astype(jnp.float32)
    grad_tokens = (dx_expert + jnp.dot(d_logits, router_float.T, precision=highest)).astype(
        jnp.bfloat16
    )
    router_part = jnp.einsum("te,tf->ef", d_logits, tokens.astype(jnp.float32), precision=highest)
    for name in reversed(EXPERT_AXES):
        router_part = lax.psum(router_part, name)
    grad_router = router_part.T
    return (mixed, grad_tokens, grad_router, grad_gate[None], grad_up[None], grad_down[None])


def expert_shape(devices):
    try:
        xs = sorted({d.coords[0] for d in devices.flat})
        zs = sorted({d.coords[2] for d in devices.flat})
        cores = sorted({d.core_on_chip for d in devices.flat})
        shape = (len(xs), len(zs), len(cores))
    except AttributeError:
        shape = (4, 8, 2)
    if int(np.prod(shape)) != devices.shape[1]:
        shape = (devices.shape[1] // 16, 8, 2)
    return shape


def solution(mesh):
    devices = mesh.devices
    fine = Mesh(
        devices.reshape((devices.shape[0],) + expert_shape(devices)), ("section",) + EXPERT_AXES
    )
    ex = EXPERT_AXES
    in_specs = (
        P(ex, "section"),
        P(ex, "section"),
        P(ex, None),
        P("section", None),
        P(ex, None, "section"),
        P(ex, None, "section"),
        P(ex, "section", None),
    )
    out_specs = (
        P(ex, "section"),
        P(ex, "section"),
        P("section", None),
        P(ex, None, "section"),
        P(ex, None, "section"),
        P(ex, "section", None),
    )
    return jax.shard_map(
        per_device, mesh=fine, in_specs=in_specs, out_specs=out_specs, check_vma=False
    )
```

profile of v0, /device:TPU:8, one launch (start us, length us, event | category | flops | bytes accessed | tf_op | source)
XLA Modules:
  0.0 387.1 jit_solution(12677243295857633148)
XLA Ops:
  7.2 1.0 fusion.58
  8.2 9.9 %psum.35 = f32[16,8]{0,1:T(8,128)S(1)} all-reduce(f32[16,8]{0,1:T(8,128)S(1)} %fusion.58), channel_id=1, replica_groups=mesh['section'=4,'ex'=4,'ez'=8,'ec'=2] {'section'}, use_global_device_ids=true, to_apply=%region_0.0 | all-reduce | flops 128 | bytes 1024 | tf_op jit(solution)/shard_map/psum | solution.py:29
  20.9 1.0 convolution_convert_fusion.3
  22.0 1.0 fusion.31
  23.1 1.0 fusion.19
  25.0 50.1 %all_to_all.10 = bf16[64,96,128]{2,1,0:T(8,128)(2,1)} all-to-all(bf16[64,96,128]{2,1,0:T(8,128)(2,1)S(1)} %bitcast.103), channel_id=1, replica_groups=mesh['section'=4,'ex'=4,'ez'=8,'ec'=2] {'ex','ez','ec'}, dimensions={0} | all-to-all | bytes 3145728 | tf_op jit(solution)/shard_map/all_to_all | solution.py:70
  75.1 4.3 %reshape.44 = bf16[64,2,6,1024]{3,2,1,0:T(8,128)(2,1)} reshape(bf16[64,96,128]{2,1,0:T(8,128)(2,1)} %all_to_all.10) | data formatting | bytes 3145728 | tf_op jit(solution)/shard_map/reshape | solution.py:72
  79.5 4.4 %copy.48 = bf16[2,64,6,1024]{3,0,2,1:T(2,128)(2,1)} copy(bf16[2,64,6,1024]{3,2,0,1:T(8,128)(2,1)} %bitcast.100) | data formatting | bytes 3145728 | tf_op jit(solution)/shard_map/transpose | solution.py:72
  83.9 4.5 %reshape_squeeze.15 = bf16[256,4,1024]{2,1,0:T(4,128)(2,1)} reshape(bf16[1,256,4096]{2,1,0:T(8,128)(2,1)} %param.13) | data formatting | bytes 4194304 | tf_op jit(solution)/shard_map/reshape;squeeze | solution.py:100
  88.4 63.9 %all-gather.2.cloned.1.call-done = bf16[2,384,4096]{2,0,1:T(2,128)(2,1)} async-done(((bf16[2,384,1024]{2,0,1:T(2,128)(2,1)}), bf16[2,384,4096]{2,0,1:T(2,128)(2,1)}) %all-gather.2.cloned.1.call-update) | async-done | bytes 6291472 | tf_op jit(solution)/shard_map/all_gather | solution.py:74
  152.3 15.7 %fusion.56 = (bf16[1,384,4096]{2,0,1:T(2,128)(2,1)S(1)}, bf16[1,384,4096]{2,0,1:T(2,128)(2,1)S(1)}) fusion(bf16[2,384,4096]{2,0,1:T(2,128)(2,1)} %all-gather.2.cloned.1.call-done), kind=kLoop, calls=%fused_computation.89 | loop fusion | bytes 12582912 | tf_op jit(solution)/shard_map/slice | solution.py:76
  168.0 3.7 copy.52
  171.7 3.6 fusion.5
  176.4 1.1 multiply_convert_fusion.2
  178.0 1.7 convert_bitcast_fusion
  180.7 1.4 fusion.3
  182.7 3.4 copy.50
  186.1 67.1 %reduce-scatter.2.cloned.1.call-done = bf16[768,1024]{1,0:T(8,128)(2,1)} async-done(((bf16[3072,1024]{1,0:T(8,128)(2,1)}), bf16[768,1024]{1,0:T(8,128)(2,1)}) %reduce-scatter.2.cloned.1.call-update) | async-done | bytes 1572880 | tf_op jit(solution)/shard_map/reduce_scatter | solution.py:112
  253.2 2.5 reshape.46
  255.7 1.6 copy.51
  257.3 4.4 %reshape.47 = bf16[64,96,128]{2,1,0:T(8,128)(2,1)} reshape(bf16[64,2,6,1024]{3,2,1,0:T(8,128)(2,1)} %copy.51) | data formatting | bytes 3145728 | tf_op jit(solution)/shard_map/reshape | solution.py:115
  261.7 10.7 %all-to-all-start.1 = ((bf16[64,96,128]{2,1,0:T(8,128)(2,1)}), bf16[64,96,128]{2,1,0:T(8,128)(2,1)}, u32[]{:S(2)}, u32[]{:S(2)}) async-start(bf16[64,96,128]{2,1,0:T(8,128)(2,1)} %reshape.47), calls=%async_computation.2 | async-start | bytes 3145728 | tf_op jit(solution)/shard_map/all_to_all | solution.py:116
  272.4 8.2 %fusion.2 = bf16[1,256,4096]{2,1,0:T(8,128)(2,1)} fusion(bf16[384,256]{1,0:T(8,128)(2,1)S(1)} %get-tuple-element.10, bf16[1,384,4096]{2,0,1:T(2,128)(2,1)} %copy-done.2), kind=kOutput, calls=%fused_computation.7 | convolution fusion | flops 806354944 | bytes 5439488 | tf_op jit(solution)/shard_map/pf,pd->fd/dot_general | solution.py:86
  280.6 2.6 fusion
  283.2 2.6 fusion.1
  285.8 25.9 %all-to-all-done.1 = bf16[64,96,128]{2,1,0:T(8,128)(2,1)} async-done(((bf16[64,96,128]{2,1,0:T(8,128)(2,1)}), bf16[64,96,128]{2,1,0:T(8,128)(2,1)}, u32[]{:S(2)}, u32[]{:S(2)}) %all-to-all-start.1) | async-done | bytes 1572896 | tf_op jit(solution)/shard_map/all_to_all | solution.py:116
  311.7 4.7 %reshape.48 = f32[8,8,2,6,1024]{4,3,2,1,0:T(8,128)} reshape(bf16[64,96,128]{2,1,0:T(8,128)(2,1)} %all-to-all-done.1) | data formatting | bytes 4718592 | tf_op jit(solution)/shard_map/convert_element_type | solution.py:117
  316.4 2.7 reduce_sum.47
  321.0 9.5 %psum.36 = f32[16,2]{0,1:T(2,128)S(1)} all-reduce(f32[16,2]{0,1:T(2,128)S(1)} %pad_maximum_fusion.2), channel_id=1, replica_groups=mesh['section'=4,'ex'=4,'ez'=8,'ec'=2] {'section'}, use_global_device_ids=true, to_apply=%region_8.9 | all-reduce | flops 32 | bytes 256 | tf_op jit(solution)/shard_map/psum | solution.py:131
  331.5 3.4 psum.37
  334.9 28.5 %psum.38 = f32[8,1024]{1,0:T(8,128)S(1)} all-reduce(f32[8,1024]{1,0:T(8,128)S(1)} %psum.37), channel_id=1, replica_groups=mesh['section'=4,'ex'=4,'ez'=8,'ec'=2] {'ez'}, use_global_device_ids=true, to_apply=%region_10.11 | all-reduce | flops 8192 | bytes 65536 | tf_op jit(solution)/shard_map/psum | solution.py:144
  363.3 16.9 %psum.39 = f32[1024,8]{0,1:T(8,128)} all-reduce(f32[1024,8]{0,1:T(8,128)S(1)} %bitcast.105), channel_id=1, replica_groups=mesh['section'=4,'ex'=4,'ez'=8,'ec'=2] {'ex'}, use_global_device_ids=true, to_apply=%region_11.12 | all-reduce | flops 8192 | bytes 65536 | tf_op jit(solution)/shard_map/psum | solution.py:144
  (59 shorter events, 9.7 us)
Async XLA Ops:
  7.2 169.2 %copy-start = (bf16[1,4096,256]{2,1,0:T(8,128)(2,1)S(1)}, bf16[1,4096,256]{2,1,0:T(8,128)(2,1)}, u32[]{:S(2)}) copy-start(bf16[1,4096,256]{2,1,0:T(8,128)(2,1)} %param.12) | copy-start | bytes 6291460
  7.2 145.1 %all-gather.2.cloned.1.call-start = ((), (), s32[]{:S(2)}) async-start(), calls=%async_computation.3 | async-start | bytes 7864320 | tf_op jit(solution)/shard_map/all_gather | solution.py:74
  83.8 169.4 %reduce-scatter.2.cloned.1.call-start = ((), (), s32[]{:S(2)}) async-start(), calls=%async_computation.4 | async-start | bytes 7864320 | tf_op jit(solution)/shard_map/reduce_scatter | solution.py:112
  168.0 3.7 copy-start.2
  168.0 3.7 copy-start.6
  171.7 4.7 %copy-start.4 = (bf16[1,384,4096]{2,1,0:T(8,128)(2,1)}, bf16[1,384,4096]{2,1,0:T(8,128)(2,1)S(1)}, u32[]{:S(2)}) copy-start(bf16[1,384,4096]{2,1,0:T(8,128)(2,1)S(1)} %copy.52) | copy-start | bytes 9437188
  171.7 3.6 copy-start.7
  176.4 1.6 copy-start.3
  257.3 15.1 %copy-start.11 = (s32[16,2]{0,1:T(2,128)S(1)}, s32[16,2]{0,1:T(2,128)}, u32[]{:S(2)}) copy-start(s32[16,2]{0,1:T(2,128)} %param.9) | copy-start | bytes 388
  261.7 50.0 %all-to-all-start.1 = ((bf16[64,96,128]{2,1,0:T(8,128)(2,1)}), bf16[64,96,128]{2,1,0:T(8,128)(2,1)}, u32[]{:S(2)}, u32[]{:S(2)}) async-start(bf16[64,96,128]{2,1,0:T(8,128)(2,1)} %reshape.47), calls=%async_computation.2 | async-start | bytes 3145728 | tf_op jit(solution)/shard_map/all_to_all | solution.py:116
  272.3 8.3 %copy-start.5 = (bf16[1,384,4096]{2,1,0:T(8,128)(2,1)S(1)}, bf16[1,384,4096]{2,1,0:T(8,128)(2,1)}, u32[]{:S(2)}) copy-start(bf16[1,384,4096]{2,1,0:T(8,128)(2,1)} %copy-done.4) | copy-start | bytes 9437188
  311.7 68.5 %copy-start.1 = (bf16[1,4096,256]{2,1,0:T(8,128)(2,1)S(1)}, bf16[1,4096,256]{2,1,0:T(8,128)(2,1)}, u32[]{:S(2)}) copy-start(bf16[1,4096,256]{2,1,0:T(8,128)(2,1)} %param.12) | copy-start | bytes 6291460
  316.4 3.6 copy-start.8
  316.4 14.1 %copy-start.9 = (bf16[16,1024]{1,0:T(8,128)(2,1)S(1)}, bf16[16,1024]{1,0:T(8,128)(2,1)}, u32[]{:S(2)}) copy-start(bf16[16,1024]{1,0:T(8,128)(2,1)} %param.7) | copy-start | bytes 98308
  316.4 14.2 %copy-start.10 = (bf16[1024,8]{0,1:T(8,128)(2,1)S(1)}, bf16[1024,8]{0,1:T(8,128)(2,1)}, u32[]{:S(2)}) copy-start(bf16[1024,8]{0,1:T(8,128)(2,1)} %param.10) | copy-start | bytes 49156
Sparse Core Ops, SparseCore 0:
  84.0 68.2 all-gather.1
  186.2 66.9 reduce-scatter.1
where the time goes:
time: 388 us; the launch traced here: 387 us
  waiting for transfers between devices  157 us (40%)
  blocking collectives  118 us (30%)
  local copies, waits for them, and re-layouts  51.2 us (13%)
  matrix products  30 us (8%)
  between operations  14.4 us (4%)
  starting transfers between devices  10.7 us (3%)
  other arithmetic  5.51 us (1%)
    reduce_scatter x1, waiting for transfers between devices, per_device(): lax.psum_scatter(pieces, 'section', scatter_dimension=0, tiled=True)  67.1 us
    all_gather x1, waiting for transfers between devices, per_device(): gathered = lax.all_gather(received, 'section', axis=2, tiled=True)  63.9 us
    all_to_all x1, blocking collectives, per_device(): received = lax.all_to_all(sent, EXPERT_AXES, 0, 0, tiled=True)  50.1 us
    psum x3, blocking collectives, per_device(): router_part = lax.psum(router_part, name)  48.7 us
    all_to_all x1, waiting for transfers between devices, per_device(): returned = lax.all_to_all(back, EXPERT_AXES, 0, 0, tiled=True)  25.9 us
    slice x1, local copies, waits for them, and re-layouts, per_device(): dy_rows = gathered[1]  15.7 us
    all_to_all x1, starting transfers between devices, per_device(): returned = lax.all_to_all(back, EXPERT_AXES, 0, 0, tiled=True)  10.7 us
    psum x1, blocking collectives, per_device(): logits = lax.psum(partial_logits, 'section')  9.88 us
  transfers between devices with their start and end apart: 3, of which 3 were waited for; matrix products, arithmetic and copies ran while one was open for 5% of the time, Pallas kernels for 0%

commit v1 on v0

--- a/solution.py
+++ b/solution.py
@@ -71,7 +71,8 @@
     row_total = received.shape[0] * capacity
     received = received.reshape(-1, 2, capacity, width).transpose(1, 0, 2, 3)
     received = received.reshape(2, row_total, width)
-    gathered = lax.all_gather(received, "section", axis=2, tiled=True)
+    outgoing = jnp.stack([received] * lax.axis_size("section"))
+    gathered = jnp.concatenate(lax.all_to_all(outgoing, "section", 0, 0), axis=2)
     x_rows = gathered[0]
     dy_rows = gathered[1]
     gate_local = w_gate[0]

time: 388 us -> 386 us (level)
  starting transfers between devices: 10.7 us -> 18.6 us
  matrix products: 30 us -> 23.6 us
    all_to_all x0 -> x1, waiting for transfers between devices: none -> 66.2 us  [per_device(): lax.all_to_all(outgoing, 'section', 0, 0)]
    all_gather x1 -> x0, waiting for transfers between devices: 63.9 us -> none  [per_device(): gathered = lax.all_gather(received, 'section', axis=2, tiled=True)]
    slice x1, local copies, waits for them, and re-layouts: 15.7 us -> 0.66 us  [per_device(): dy_rows = gathered[1]]
    another operation x0 -> x2, local copies, waits for them, and re-layouts: none -> 9.52 us  [per_device(): outgoing = jnp.stack([received] * lax.axis_size('section'))]
    all_to_all x0 -> x1, starting transfers between devices: none -> 7.69 us  [per_device(): lax.all_to_all(outgoing, 'section', 0, 0)]
    reduce_scatter x1, waiting for transfers between devices: 67.1 us -> 61.3 us  [per_device(): lax.psum_scatter(pieces, 'section', scatter_dimension=0, tiled=True)]
  transfers between devices with their start and end apart: 3 -> 3, of which waited for: 3 -> 3; matrix products, arithmetic and copies ran while one was open for 5% -> 4% of each run, Pallas kernels for 0% -> 0%
where the time goes in v1:
time: 386 us; the launch traced here: 385 us
  waiting for transfers between devices  157 us (41%)
  blocking collectives  118 us (31%)
  local copies, waits for them, and re-layouts  47.7 us (12%)
  matrix products  23.6 us (6%)
  starting transfers between devices  18.6 us (5%)
  between operations  14.3 us (4%)
  other arithmetic  5.51 us (1%)
    all_to_all x1, waiting for transfers between devices, per_device(): lax.all_to_all(outgoing, 'section', 0, 0)  66.2 us
    reduce_scatter x1, waiting for transfers between devices, per_device(): lax.psum_scatter(pieces, 'section', scatter_dimension=0, tiled=True)  61.3 us
    all_to_all x1, blocking collectives, per_device(): received = lax.all_to_all(sent, EXPERT_AXES, 0, 0, tiled=True)  50.1 us
    psum x3, blocking collectives, per_device(): router_part = lax.psum(router_part, name)  48.7 us
    all_to_all x1, waiting for transfers between devices, per_device(): returned = lax.all_to_all(back, EXPERT_AXES, 0, 0, tiled=True)  29.3 us
    all_to_all x1, starting transfers between devices, per_device(): returned = lax.all_to_all(back, EXPERT_AXES, 0, 0, tiled=True)  10.9 us
    psum x1, blocking collectives, per_device(): logits = lax.psum(partial_logits, 'section')  9.88 us
    another operation x2, local copies, waits for them, and re-layouts, per_device(): outgoing = jnp.stack([received] * lax.axis_size('section'))  9.52 us
  transfers between devices with their start and end apart: 3, of which 3 were waited for; matrix products, arithmetic and copies ran while one was open for 4% of the time, Pallas kernels for 0%

profile of v1, /device:TPU:8, one launch (start us, length us, event | category | flops | bytes accessed | tf_op | source)
XLA Modules:
  0.0 384.9 jit_solution(4120969256749700925)
XLA Ops:
  8.2 9.9 %psum.35 = f32[16,8]{0,1:T(8,128)S(1)} all-reduce(f32[16,8]{0,1:T(8,128)S(1)} %fusion.50), channel_id=1, replica_groups=mesh['section'=4,'ex'=4,'ez'=8,'ec'=2] {'section'}, use_global_device_ids=true, to_apply=%region_0.0 | all-reduce | flops 128 | bytes 1024 | tf_op jit(solution)/shard_map/psum | solution.py:29
  25.0 50.1 %all_to_all.15 = bf16[64,96,128]{2,1,0:T(8,128)(2,1)} all-to-all(bf16[64,96,128]{2,1,0:T(8,128)(2,1)S(1)} %bitcast.104), channel_id=1, replica_groups=mesh['section'=4,'ex'=4,'ez'=8,'ec'=2] {'ex','ez','ec'}, dimensions={0} | all-to-all | bytes 3145728 | tf_op jit(solution)/shard_map/all_to_all | solution.py:70
  75.1 4.3 %reshape.51 = bf16[64,2,6,1024]{3,2,1,0:T(8,128)(2,1)} reshape(bf16[64,96,128]{2,1,0:T(8,128)(2,1)} %all_to_all.15) | data formatting | bytes 3145728 | tf_op jit(solution)/shard_map/reshape | solution.py:72
  79.4 4.4 %copy.42 = bf16[2,64,6,1024]{3,0,2,1:T(2,128)(2,1)} copy(bf16[2,64,6,1024]{3,2,0,1:T(8,128)(2,1)} %bitcast.102) | data formatting | bytes 3145728 | tf_op jit(solution)/shard_map/transpose | solution.py:72
  83.8 4.9 %copy.43 = bf16[2,384,1024]{1,2,0:T(8,128)(2,1)} copy(bf16[2,384,1024]{2,0,1:T(2,128)(2,1)} %bitcast.105) | data formatting | bytes 3145728 | tf_op jit(solution)/shard_map/stack;reshape | solution.py:74
  88.7 4.6 %stack.28 = bf16[4,2,384,1024]{2,3,1,0:T(8,128)(2,1)} broadcast(bf16[2,384,1024]{1,2,0:T(8,128)(2,1)} %copy.43), dimensions={1,2,3} | broadcast | bytes 7864320 | tf_op jit(solution)/shard_map/stack | solution.py:74
  93.3 7.7 %all-to-all-start.1 = ((bf16[4,2,384,1024]{2,3,1,0:T(8,128)(2,1)}), bf16[4,2,384,1024]{2,3,1,0:T(8,128)(2,1)}, u32[]{:S(2)}, u32[]{:S(2)}) async-start(bf16[4,2,384,1024]{2,3,1,0:T(8,128)(2,1)} %stack.28), calls=%async_computation.1 | async-start | bytes 12582912 | tf_op jit(solution)/shard_map/all_to_all | solution.py:75
  101.0 4.5 %reshape_squeeze.15 = bf16[256,4,1024]{2,1,0:T(4,128)(2,1)} reshape(bf16[1,256,4096]{2,1,0:T(8,128)(2,1)} %param.13) | data formatting | bytes 4194304 | tf_op jit(solution)/shard_map/reshape;squeeze | solution.py:101
  105.5 66.2 %all-to-all-done.1 = bf16[4,2,384,1024]{2,3,1,0:T(8,128)(2,1)} async-done(((bf16[4,2,384,1024]{2,3,1,0:T(8,128)(2,1)}), bf16[4,2,384,1024]{2,3,1,0:T(8,128)(2,1)}, u32[]{:S(2)}, u32[]{:S(2)}) %all-to-all-start.1) | async-done | bytes 6291488 | tf_op jit(solution)/shard_map/all_to_all | solution.py:75
  171.7 3.4 copy.51
  176.7 1.1 fusion.4
  177.8 1.4 copy-done.7
  179.2 1.1 fusion.8
  180.3 1.1 multiply_convert_fusion.2
  181.9 1.7 convert_bitcast_fusion
  184.6 1.2 fusion.3
  186.3 3.4 copy.46
  189.7 61.3 %reduce-scatter.2.cloned.1.call-done = bf16[768,1024]{1,0:T(8,128)(2,1)} async-done(((bf16[3072,1024]{1,0:T(8,128)(2,1)}), bf16[768,1024]{1,0:T(8,128)(2,1)}) %reduce-scatter.2.cloned.1.call-update) | async-done | bytes 1572880 | tf_op jit(solution)/shard_map/reduce_scatter | solution.py:113
  251.0 2.5 reshape.53
  253.5 1.6 copy.47
  255.1 4.4 %reshape.54 = bf16[64,96,128]{2,1,0:T(8,128)(2,1)} reshape(bf16[64,2,6,1024]{3,2,1,0:T(8,128)(2,1)} %copy.47) | data formatting | bytes 3145728 | tf_op jit(solution)/shard_map/reshape | solution.py:116
  259.4 10.9 %all-to-all-start.2 = ((bf16[64,96,128]{2,1,0:T(8,128)(2,1)}), bf16[64,96,128]{2,1,0:T(8,128)(2,1)}, u32[]{:S(2)}, u32[]{:S(2)}) async-start(bf16[64,96,128]{2,1,0:T(8,128)(2,1)} %reshape.54), calls=%async_computation.3 | async-start | bytes 3145728 | tf_op jit(solution)/shard_map/all_to_all | solution.py:117
  270.4 4.7 %fusion.2 = bf16[1,256,4096]{2,1,0:T(8,128)(2,1)} fusion(bf16[384,256]{1,0:T(8,128)(2,1)S(1)} %get-tuple-element.10, bf16[384,4096]{0,1:T(8,128)(2,1)} %bitcast.101), kind=kOutput, calls=%fused_computation.8 | convolution fusion | flops 806354944 | bytes 5439488 | tf_op jit(solution)/shard_map/pf,pd->fd/dot_general | solution.py:87
  275.0 2.6 fusion
  277.6 2.6 fusion.1
  280.2 29.3 %all-to-all-done.2 = bf16[64,96,128]{2,1,0:T(8,128)(2,1)} async-done(((bf16[64,96,128]{2,1,0:T(8,128)(2,1)}), bf16[64,96,128]{2,1,0:T(8,128)(2,1)}, u32[]{:S(2)}, u32[]{:S(2)}) %all-to-all-start.2) | async-done | bytes 1572896 | tf_op jit(solution)/shard_map/all_to_all | solution.py:117
  309.5 4.7 %reshape.55 = f32[8,8,2,6,1024]{4,3,2,1,0:T(8,128)} reshape(bf16[64,96,128]{2,1,0:T(8,128)(2,1)} %all-to-all-done.2) | data formatting | bytes 4718592 | tf_op jit(solution)/shard_map/convert_element_type | solution.py:118
  314.2 2.7 reduce_sum.47
  318.8 9.5 %psum.36 = f32[16,2]{0,1:T(2,128)S(1)} all-reduce(f32[16,2]{0,1:T(2,128)S(1)} %pad_maximum_fusion.2), channel_id=1, replica_groups=mesh['section'=4,'ex'=4,'ez'=8,'ec'=2] {'section'}, use_global_device_ids=true, to_apply=%region_8.9 | all-reduce | flops 32 | bytes 256 | tf_op jit(solution)/shard_map/psum | solution.py:132
  329.3 3.4 psum.37
  332.7 28.5 %psum.38 = f32[8,1024]{1,0:T(8,128)S(1)} all-reduce(f32[8,1024]{1,0:T(8,128)S(1)} %psum.37), channel_id=1, replica_groups=mesh['section'=4,'ex'=4,'ez'=8,'ec'=2] {'ez'}, use_global_device_ids=true, to_apply=%region_10.11 | all-reduce | flops 8192 | bytes 65536 | tf_op jit(solution)/shard_map/psum | solution.py:145
  361.2 16.9 %psum.39 = f32[1024,8]{0,1:T(8,128)} all-reduce(f32[1024,8]{0,1:T(8,128)S(1)} %bitcast.107), channel_id=1, replica_groups=mesh['section'=4,'ex'=4,'ez'=8,'ec'=2] {'ex'}, use_global_device_ids=true, to_apply=%region_11.12 | all-reduce | flops 8192 | bytes 65536 | tf_op jit(solution)/shard_map/psum | solution.py:145
  (60 shorter events, 14.3 us)
Async XLA Ops:
  7.2 173.1 %copy-start = (bf16[1,4096,256]{2,1,0:T(8,128)(2,1)S(1)}, bf16[1,4096,256]{2,1,0:T(8,128)(2,1)}, u32[]{:S(2)}) copy-start(bf16[1,4096,256]{2,1,0:T(8,128)(2,1)} %param.12) | copy-start | bytes 6291460
  93.3 78.4 %all-to-all-start.1 = ((bf16[4,2,384,1024]{2,3,1,0:T(8,128)(2,1)}), bf16[4,2,384,1024]{2,3,1,0:T(8,128)(2,1)}, u32[]{:S(2)}, u32[]{:S(2)}) async-start(bf16[4,2,384,1024]{2,3,1,0:T(8,128)(2,1)} %stack.28), calls=%async_computation.1 | async-start | bytes 12582912 | tf_op jit(solution)/shard_map/all_to_all | solution.py:75
  101.0 150.0 %reduce-scatter.2.cloned.1.call-start = ((), (), s32[]{:S(2)}) async-start(), calls=%async_computation.4 | async-start | bytes 7864320 | tf_op jit(solution)/shard_map/reduce_scatter | solution.py:113
  175.1 1.6 copy-start.6
  175.8 4.4 %copy-start.2 = (bf16[1,384,4,1024]{1,3,2,0:T(8,128)(2,1)}, bf16[1,384,4,1024]{1,3,2,0:T(8,128)(2,1)S(1)}, u32[]{:S(2)}) copy-start(bf16[1,384,4,1024]{1,3,2,0:T(8,128)(2,1)S(1)} %get-tuple-element.9) | copy-start | bytes 9437188
  175.8 4.4 %copy-start.4 = (bf16[1,384,4,1024]{1,3,2,0:T(8,128)(2,1)}, bf16[1,384,4,1024]{1,3,2,0:T(8,128)(2,1)S(1)}, u32[]{:S(2)}) copy-start(bf16[1,384,4,1024]{1,3,2,0:T(8,128)(2,1)S(1)} %get-tuple-element.8) | copy-start | bytes 9437188
  175.8 3.3 copy-start.7
  180.3 1.6 copy-start.5
  255.1 15.3 %copy-start.11 = (s32[16,2]{0,1:T(2,128)S(1)}, s32[16,2]{0,1:T(2,128)}, u32[]{:S(2)}) copy-start(s32[16,2]{0,1:T(2,128)} %param.9) | copy-start | bytes 388
  259.4 50.1 %all-to-all-start.2 = ((bf16[64,96,128]{2,1,0:T(8,128)(2,1)}), bf16[64,96,128]{2,1,0:T(8,128)(2,1)}, u32[]{:S(2)}, u32[]{:S(2)}) async-start(bf16[64,96,128]{2,1,0:T(8,128)(2,1)} %reshape.54), calls=%async_computation.3 | async-start | bytes 3145728 | tf_op jit(solution)/shard_map/all_to_all | solution.py:117
  270.4 4.7 %copy-start.3 = (bf16[1,384,4,1024]{1,3,2,0:T(8,128)(2,1)S(1)}, bf16[1,384,4,1024]{1,3,2,0:T(8,128)(2,1)}, u32[]{:S(2)}) copy-start(bf16[1,384,4,1024]{1,3,2,0:T(8,128)(2,1)} %copy-done.2) | copy-start | bytes 9437188
  309.5 68.5 %copy-start.1 = (bf16[1,4096,256]{2,1,0:T(8,128)(2,1)S(1)}, bf16[1,4096,256]{2,1,0:T(8,128)(2,1)}, u32[]{:S(2)}) copy-start(bf16[1,4096,256]{2,1,0:T(8,128)(2,1)} %param.12) | copy-start | bytes 6291460
  314.2 3.6 copy-start.8
  314.2 14.1 %copy-start.9 = (bf16[16,1024]{1,0:T(8,128)(2,1)S(1)}, bf16[16,1024]{1,0:T(8,128)(2,1)}, u32[]{:S(2)}) copy-start(bf16[16,1024]{1,0:T(8,128)(2,1)} %param.7) | copy-start | bytes 98308
  314.2 14.2 %copy-start.10 = (bf16[1024,8]{0,1:T(8,128)(2,1)S(1)}, bf16[1024,8]{0,1:T(8,128)(2,1)}, u32[]{:S(2)}) copy-start(bf16[1024,8]{0,1:T(8,128)(2,1)} %param.10) | copy-start | bytes 49156
Sparse Core Ops, SparseCore 0:
  189.9 61.1 reduce-scatter.1
